TPU v7x, 512 devices: a whole 4x4x16 slice. The times are simulated.
512 devices in a mesh: dp: 32 (over y, z_lo, core), ctx: 16 (over x, z_hi).
Axes of the slice: x: 4, y: 4, z: 16 (z_hi: 4, z_lo: 4; z = z_hi * 4 + z_lo), core: 2. Of those that a mesh axis runs over, the one named last changes fastest.
Arguments:
- branch_in: bfloat16 [32, 2048, 2816], P('dp', 'ctx'), may hold values from -6 to 6
- cotangent: bfloat16 [32, 2048, 2816], P('dp', 'ctx'), may hold values from -6 to 6
- weight_a: bfloat16 [256, 2816], P('dp', 'ctx'), may hold values from -0.375 to 0.375
- weight_x: bfloat16 [256, 2816], P('dp', 'ctx'), may hold values from -0.375 to 0.375
- conv_weight: bfloat16 [4, 2816], P(None, 'ctx'), may hold values from -3 to 3
- conv_bias: bfloat16 [2816], P('ctx'), may hold values from -3 to 3
- bias_a: bfloat16 [2816], P('ctx'), may hold values from -4 to 4
- bias_x: bfloat16 [2816], P('ctx'), may hold values from -4 to 4
- rate: bfloat16 [2816], P('ctx'), may hold values from 0 to 0.016, as said below
Outputs:
- grad_input: bfloat16 [32, 2048, 2816], P('dp', 'ctx')
- grad_weight_a: float32 [256, 2816], P('dp', 'ctx')
- grad_rate: float32 [2816], replicated
Inputs may be any that keep to these rules, and one draw needn't show every extreme that they name: `rate`: positive in every channel.
All inputs are finite; a program needn't handle non-finite values.
Results may differ from a plain program's by a relative error of at most 0.006.
Values may be sent and summed in bfloat16 or wider, within the bound.
No kernel may reach another device: no remote copies, remote signals or barrier semaphores. Data moves between devices by JAX's collectives and lax.ppermute only.
A program may use at most 128 MiB of HBM per device.

v0:
```python
import math
import jax
import jax.numpy as jnp
from jax import lax
from jax.sharding import PartitionSpec as P

floor_value = 2.5e-07


def passed_along(array, axis, by):
    length = lax.axis_size(axis)
    pairs = [(i, i + by) for i in range(length) if 0 <= i + by < length]
    return lax.ppermute(array, axis, pairs)


def mix_heads(values, weights):
    tokens = values.shape[0]
    head_width = weights.shape[0]
    head_count = weights.shape[1] // head_width
    left = values.reshape(tokens, head_count, head_width)
    right = weights.reshape(head_width, head_count, head_width)
    result = jnp.einsum("thk,khj->thj", left, right, preferred_element_type=jnp.float32)
    return result.reshape(tokens, head_count * head_width)


def back_heads(grads, weights):
    tokens = grads.shape[0]
    head_width = weights.shape[0]
    head_count = weights.shape[1] // head_width
    left = grads.reshape(tokens, head_count, head_width)
    right = weights.reshape(head_width, head_count, head_width)
    result = jnp.einsum("thj,khj->thk", left, right, preferred_element_type=jnp.float32)
    return result.reshape(tokens, head_count * head_width)


def grad_heads(values, grads, head_width):
    tokens = values.shape[0]
    head_count = values.shape[1] // head_width
    left = values.reshape(tokens, head_count, head_width)
    right = grads.reshape(tokens, head_count, head_width)
    result = jnp.einsum("thk,thj->khj", left, right, preferred_element_type=jnp.float32)
    return result.reshape(head_width, head_count * head_width)


def combine(earlier, later):
    return (earlier[0] * later[0], later[0] * earlier[1] + later[1])


def block_scan(coef, value, reverse):
    length = coef.shape[0]
    width = coef.shape[1]
    block_size = math.gcd(length, 16)
    block_count = length // block_size
    coef_blocks = coef.reshape(block_count, block_size, width)
    value_blocks = value.reshape(block_count, block_size, width)
    visit_order = list(range(block_size))
    if reverse:
        visit_order = visit_order[::-1]
    coef_rows = [None] * block_size
    value_rows = [None] * block_size
    running_coef = None
    running_value = None
    for position in visit_order:
        step_coef = coef_blocks[:, position]
        step_value = value_blocks[:, position]
        if running_coef is None:
            running_coef = step_coef
            running_value = step_value
        else:
            running_value = step_coef * running_value + step_value
            running_coef = running_coef * step_coef
        coef_rows[position] = running_coef
        value_rows[position] = running_value
    local_coef = jnp.stack(coef_rows, 1)
    local_value = jnp.stack(value_rows, 1)
    edge = 0 if reverse else block_size - 1
    summary_coef = local_coef[:, edge]
    summary_value = local_value[:, edge]
    incl_coef, incl_value = lax.associative_scan(
        combine, (summary_coef, summary_value), reverse=reverse, axis=0
    )
    ones_row = jnp.ones((1, width), jnp.float32)
    zero_row = jnp.zeros((1, width), jnp.float32)
    if reverse:
        prior_coef = jnp.concatenate([incl_coef[1:], ones_row], 0)
        prior_value = jnp.concatenate([incl_value[1:], zero_row], 0)
    else:
        prior_coef = jnp.concatenate([ones_row, incl_coef[:-1]], 0)
        prior_value = jnp.concatenate([zero_row, incl_value[:-1]], 0)
    whole_coef = local_coef * prior_coef[:, None]
    whole_value = local_coef * prior_value[:, None] + local_value
    return (whole_coef.reshape(length, width), whole_value.reshape(length, width))


def on_device(
    branch_in, cotangent, weight_a, weight_x, conv_weight, conv_bias, bias_a, bias_x, rate
):
    inputs = branch_in[0]
    upstream = cotangent[0].astype(jnp.float32)
    length = inputs.shape[0]
    taps = conv_weight.shape[0]
    packed = jnp.concatenate(
        [conv_weight, conv_bias[None], bias_a[None], bias_x[None], rate[None]], 0
    )
    rows_a, rows_x = (
        lax.all_gather(weight_a, "dp", axis=0, tiled=True),
        lax.all_gather(weight_x, "dp", axis=0, tiled=True),
    )
    full_a, full_x, params = (
        lax.all_gather(rows_a, "ctx", axis=1, tiled=True),
        lax.all_gather(rows_x, "ctx", axis=1, tiled=True),
        lax.all_gather(packed, "ctx", axis=1, tiled=True),
    )
    params = params.astype(jnp.float32)
    taps_f = params[:taps]
    cbias = params[taps]
    abias = params[taps + 1]
    xbias = params[taps + 2]
    rates = params[taps + 3]
    width = params.shape[1]
    head_width = full_a.shape[0]
    tail = passed_along(inputs[length - (taps - 1) :], "ctx", 1)
    padded = jnp.concatenate([tail, inputs], 0).astype(jnp.float32)
    conv = cbias
    for tap in range(taps):
        conv = conv + taps_f[tap] * padded[tap : tap + length]
    conv_b = conv.astype(jnp.bfloat16)
    conv_f = conv_b.astype(jnp.float32)
    recur_gate = jax.nn.sigmoid(mix_heads(conv_b, full_a) + abias)
    input_gate = jax.nn.sigmoid(mix_heads(conv_b, full_x) + xbias)
    log_decay = -8.0 * recur_gate * rates
    decay = jnp.exp(log_decay)
    one_minus = -jnp.expm1(2.0 * log_decay)
    multiplier = jnp.sqrt(jnp.maximum(one_minus, floor_value))
    drive = multiplier * input_gate * conv_f
    cum_decay, local_hidden = block_scan(decay, drive, False)
    zero_row = jnp.zeros((width,), jnp.float32)
    span = lax.axis_size("ctx")

    def forward_turn(turn, incoming):
        outgoing = cum_decay[-1] * incoming + local_hidden[-1]
        return passed_along(outgoing, "ctx", 1)

    state_in = lax.fori_loop(0, span - 1, forward_turn, zero_row)
    hidden = local_hidden + cum_decay * state_in
    previous = jnp.concatenate([state_in[None], hidden[:-1]], 0)
    coefs = jnp.concatenate([decay[1:], jnp.ones((1, width), jnp.float32)], 0)
    cum_coef, local_back = block_scan(coefs, upstream, True)
    head_coef = decay[0] * cum_coef[0]
    head_value = decay[0] * local_back[0]

    def backward_turn(turn, incoming):
        outgoing = head_coef * incoming + head_value
        return passed_along(outgoing, "ctx", -1)

    back_in = lax.fori_loop(0, span - 1, backward_turn, zero_row)
    back = local_back + cum_coef * back_in
    slope = jnp.where(one_minus > floor_value, 0.5 / multiplier, 0.0)
    d_mult = back * input_gate * conv_f
    d_log = back * previous * decay - 2.0 * decay * decay * d_mult * slope
    d_recur = (d_log * (-8.0 * rates) * recur_gate * (1.0 - recur_gate)).astype(jnp.bfloat16)
    d_input = (back * multiplier * conv_f * input_gate * (1.0 - input_gate)).astype(jnp.bfloat16)
    d_conv = (
        back * multiplier * input_gate + back_heads(d_recur, full_a) + back_heads(d_input, full_x)
    )
    following = passed_along(d_conv[: taps - 1], "ctx", -1)
    dpad = jnp.concatenate([d_conv, following], 0)
    grad_in = jnp.zeros((length, width), jnp.float32)
    for tap in range(taps):
        start = taps - 1 - tap
        grad_in = grad_in + taps_f[tap] * dpad[start : start + length]
    local_wgrad = grad_heads(conv_b, d_recur, head_width)
    row_part = lax.psum_scatter(local_wgrad, "dp", scatter_dimension=0, tiled=True)
    wgrad = lax.psum_scatter(row_part, "ctx", scatter_dimension=1, tiled=True)
    rgrad = lax.psum(jnp.sum(d_log * (-8.0 * recur_gate), axis=0), ("dp", "ctx"))
    return (grad_in.astype(jnp.bfloat16)[None], wgrad, rgrad)


def solution(mesh):
    placed = (
        P("dp", "ctx", None),
        P("dp", "ctx", None),
        P("dp", "ctx"),
        P("dp", "ctx"),
        P(None, "ctx"),
        P("ctx"),
        P("ctx"),
        P("ctx"),
        P("ctx"),
    )
    return jax.shard_map(
        on_device,
        mesh=mesh,
        in_specs=placed,
        out_specs=(P("dp", "ctx", None), P("dp", "ctx"), P()),
        check_vma=False,
    )
```

profile of v0, /device:TPU:8, one launch (start us, length us, event | category | flops | bytes accessed | tf_op | source)
XLA Modules:
  0.0 1052.8 jit_solution(17856726429922451769)
XLA Ops:
  7.2 38.4 %all_gather.16 = bf16[256,176]{1,0:T(8,128)(2,1)S(1)} all-gather(bf16[8,176]{1,0:T(8,128)(2,1)} %param.15), channel_id=1, replica_groups=mesh['dp'=32,'ctx'=16] {'dp'}, dimensions={0}, use_global_device_ids=true | all-gather | bytes 92928 | tf_op jit(solution)/shard_map/all_gather | solution.py:106
  47.2 9.1 collective-permute-start.2
  56.3 38.7 %all_gather.18 = bf16[256,176]{1,0:T(8,128)(2,1)S(1)} all-gather(bf16[8,176]{1,0:T(8,128)(2,1)} %param.16), channel_id=1, replica_groups=mesh['dp'=32,'ctx'=16] {'dp'}, dimensions={0}, use_global_device_ids=true | all-gather | bytes 92928 | tf_op jit(solution)/shard_map/all_gather | solution.py:107
  99.2 55.8 %all-gather = bf16[16,176,8]{1,2,0:T(8,128)(2,1)S(1)} all-gather(bf16[1,176,8]{1,2,0:T(8,128)(2,1)S(1)} %bitcast.278), channel_id=1, replica_groups=mesh['dp'=32,'ctx'=16] {'ctx'}, dimensions={0}, use_global_device_ids=true | all-gather | bytes 47872 | tf_op jit(solution)/shard_map/all_gather | solution.py:112
  185.2 35.6 %all-gather.6.cloned.1.call-done = bf16[256,2816]{0,1:T(8,128)(2,1)} async-done(((bf16[256,176]{0,1:T(8,128)(2,1)}), bf16[256,2816]{0,1:T(8,128)(2,1)}) %all-gather.6.cloned.1.call-update) | async-done | bytes 1441808 | tf_op jit(solution)/shard_map/all_gather | solution.py:111
  270.9 10.1 slice.532
  281.0 10.1 slice.525
  291.0 10.1 slice.529
  301.1 10.1 slice.527
  392.6 166.2 %while.21 = (s32[]{:T(128)}, f32[2816]{0:T(1024)S(1)}, f32[128,2816]{1,0:T(8,128)}, f32[128,2816]{1,0:T(8,128)}, s32[]{:T(128)}) while((s32[]{:T(128)}, f32[2816]{0:T(1024)S(1)}, f32[128,2816]{1,0:T(8,128)}, f32[128,2816]{1,0:T(8,128)}, s32[]{:T(128)}) %tuple.181), condition=%wide.region_3.0_spmd, body=%wide.region_2.0_spmd.sunk | while | flops 5634 | bytes 135269 | solution.py:144
  595.8 158.0 %while.20 = (s32[]{:T(128)}, f32[2816]{0:T(1024)S(1)}, f32[2816]{0:T(1024)S(1)}, f32[2816]{0:T(1024)S(1)}, s32[]{:T(128)}) while((s32[]{:T(128)}, f32[2816]{0:T(1024)S(1)}, f32[2816]{0:T(1024)S(1)}, f32[2816]{0:T(1024)S(1)}, s32[]{:T(128)}) %tuple.169), condition=%wide.region_1.0_spmd, body=%wide.region_0.0_spmd.sunk | while | flops 5634 | bytes 90213 | solution.py:156
  597.1 9.4 collective-permute-done
  607.8 9.4 collective-permute-done
  618.5 9.8 collective-permute-done
  629.5 9.4 collective-permute-done
  640.2 9.2 collective-permute-done
  650.7 9.1 collective-permute-done
  671.4 9.5 collective-permute-done
  692.2 9.3 collective-permute-done
  702.8 9.5 collective-permute-done
  734.3 9.1 collective-permute-done
  782.9 114.6 %psum.7 = f32[2816]{0:T(1024)} all-reduce(f32[2816]{0:T(1024)S(1)} %get-tuple-element.94), channel_id=1, replica_groups=mesh['dp'=32,'ctx'=16] {'dp','ctx'}, use_global_device_ids=true, to_apply=%region_7.8 | all-reduce | flops 2816 | bytes 22528 | tf_op jit(solution)/shard_map/psum | solution.py:175
  898.0 9.7 reduce-scatter.5.cloned.1.call-done
  917.2 127.5 %reduce-scatter.7.cloned.1.call-done = f32[176,8]{1,0:T(8,128)} async-done(((f32[2816,8]{1,0:T(8,128)}), f32[176,8]{1,0:T(8,128)}) %reduce-scatter.7.cloned.1.call-update) | async-done | bytes 5648
  (492 shorter events, 474.0 us)
Async XLA Ops:
  7.2 159.0 %all-gather.4.cloned.1.call-start = ((), (), s32[]{:S(2)}) async-start(), calls=%async_computation.2 | async-start | bytes 1531904 | tf_op jit(solution)/shard_map/all_gather | solution.py:110
  46.4 174.4 %all-gather.6.cloned.1.call-start = ((), (), s32[]{:S(2)}) async-start(), calls=%async_computation.3 | async-start | bytes 1531904 | tf_op jit(solution)/shard_map/all_gather | solution.py:111
  47.2 111.4 %collective-permute-start.2 = (bf16[3,2816]{1,0:T(4,128)(2,1)S(1)}, bf16[3,2816]{1,0:T(4,128)(2,1)S(1)}, u32[]{:S(2)}, u32[]{:S(2)}) collective-permute-start(bf16[3,2816]{1,0:T(4,128)(2,1)S(1)} %slice_bitcast_fusion), channel_id=1, source_target_pairs={{0,1},{1,2},{2,3},{3,4},{4,5},{5,6},{6,7},{7,8},{8,9},{9,10},{10,1... | collective-permute-start | bytes 50696 | tf_op jit(solution)/shard_map/ppermute | solution.py:13
  95.8 811.9 %reduce-scatter.5.cloned.1.call-start = ((), (), s32[]{:S(2)}) async-start(), calls=%async_computation.4 | async-start | bytes 2973696 | tf_op jit(solution)/shard_map/reduce_scatter | solution.py:173
  434.0 9.8 collective-permute-start.1
  536.0 10.6 %collective-permute-start.1 = (f32[2816]{0:T(1024)}, f32[2816]{0:T(1024)S(1)}, u32[]{:S(2)}, u32[]{:S(2)}) collective-permute-start(f32[2816]{0:T(1024)} %multiply_add_fusion.31), channel_id=1, source_target_pairs={{0,1},{1,2},{2,3},{3,4},{4,5},{5,6},{6,7},{7,8},{8,9},{9,10},{10,1... | collective-permute-start | bytes 33800 | tf_op jit(solution)/shard_map/while/body/eval_jaxpr/ppermute | solution.py:13
  548.2 10.6 %collective-permute-start.1 = (f32[2816]{0:T(1024)}, f32[2816]{0:T(1024)S(1)}, u32[]{:S(2)}, u32[]{:S(2)}) collective-permute-start(f32[2816]{0:T(1024)} %multiply_add_fusion.31), channel_id=1, source_target_pairs={{0,1},{1,2},{2,3},{3,4},{4,5},{5,6},{6,7},{7,8},{8,9},{9,10},{10,1... | collective-permute-start | bytes 33800 | tf_op jit(solution)/shard_map/while/body/eval_jaxpr/ppermute | solution.py:13
  595.8 10.7 %collective-permute-start = (f32[2816]{0:T(1024)S(1)}, f32[2816]{0:T(1024)S(1)}, u32[]{:S(2)}, u32[]{:S(2)}) collective-permute-start(f32[2816]{0:T(1024)S(1)} %multiply_add_fusion.30), channel_id=1, source_target_pairs={{1,0},{2,1},{3,2},{4,3},{5,4},{6,5},{7,6},{8,7},{9,8},{10,9},{11,1... | collective-permute-start | bytes 33800 | tf_op jit(solution)/shard_map/while/body/eval_jaxpr/ppermute | solution.py:13
  606.5 10.7 %collective-permute-start = (f32[2816]{0:T(1024)S(1)}, f32[2816]{0:T(1024)S(1)}, u32[]{:S(2)}, u32[]{:S(2)}) collective-permute-start(f32[2816]{0:T(1024)S(1)} %multiply_add_fusion.30), channel_id=1, source_target_pairs={{1,0},{2,1},{3,2},{4,3},{5,4},{6,5},{7,6},{8,7},{9,8},{10,9},{11,1... | collective-permute-start | bytes 33800 | tf_op jit(solution)/shard_map/while/body/eval_jaxpr/ppermute | solution.py:13
  617.2 11.1 %collective-permute-start = (f32[2816]{0:T(1024)S(1)}, f32[2816]{0:T(1024)S(1)}, u32[]{:S(2)}, u32[]{:S(2)}) collective-permute-start(f32[2816]{0:T(1024)S(1)} %multiply_add_fusion.30), channel_id=1, source_target_pairs={{1,0},{2,1},{3,2},{4,3},{5,4},{6,5},{7,6},{8,7},{9,8},{10,9},{11,1... | collective-permute-start | bytes 33800 | tf_op jit(solution)/shard_map/while/body/eval_jaxpr/ppermute | solution.py:13
  628.3 10.7 %collective-permute-start = (f32[2816]{0:T(1024)S(1)}, f32[2816]{0:T(1024)S(1)}, u32[]{:S(2)}, u32[]{:S(2)}) collective-permute-start(f32[2816]{0:T(1024)S(1)} %multiply_add_fusion.30), channel_id=1, source_target_pairs={{1,0},{2,1},{3,2},{4,3},{5,4},{6,5},{7,6},{8,7},{9,8},{10,9},{11,1... | collective-permute-start | bytes 33800 | tf_op jit(solution)/shard_map/while/body/eval_jaxpr/ppermute | solution.py:13
  638.9 10.5 collective-permute-start
  649.4 10.4 collective-permute-start
  659.8 10.3 collective-permute-start
  670.1 10.7 %collective-permute-start = (f32[2816]{0:T(1024)S(1)}, f32[2816]{0:T(1024)S(1)}, u32[]{:S(2)}, u32[]{:S(2)}) collective-permute-start(f32[2816]{0:T(1024)S(1)} %multiply_add_fusion.30), channel_id=1, source_target_pairs={{1,0},{2,1},{3,2},{4,3},{5,4},{6,5},{7,6},{8,7},{9,8},{10,9},{11,1... | collective-permute-start | bytes 33800 | tf_op jit(solution)/shard_map/while/body/eval_jaxpr/ppermute | solution.py:13
  680.9 10.0 collective-permute-start
  690.9 10.6 %collective-permute-start = (f32[2816]{0:T(1024)S(1)}, f32[2816]{0:T(1024)S(1)}, u32[]{:S(2)}, u32[]{:S(2)}) collective-permute-start(f32[2816]{0:T(1024)S(1)} %multiply_add_fusion.30), channel_id=1, source_target_pairs={{1,0},{2,1},{3,2},{4,3},{5,4},{6,5},{7,6},{8,7},{9,8},{10,9},{11,1... | collective-permute-start | bytes 33800 | tf_op jit(solution)/shard_map/while/body/eval_jaxpr/ppermute | solution.py:13
  701.5 10.8 %collective-permute-start = (f32[2816]{0:T(1024)S(1)}, f32[2816]{0:T(1024)S(1)}, u32[]{:S(2)}, u32[]{:S(2)}) collective-permute-start(f32[2816]{0:T(1024)S(1)} %multiply_add_fusion.30), channel_id=1, source_target_pairs={{1,0},{2,1},{3,2},{4,3},{5,4},{6,5},{7,6},{8,7},{9,8},{10,9},{11,1... | collective-permute-start | bytes 33800 | tf_op jit(solution)/shard_map/while/body/eval_jaxpr/ppermute | solution.py:13
  712.4 10.3 collective-permute-start
  722.6 10.4 collective-permute-start
  733.0 10.4 collective-permute-start
  743.4 10.4 collective-permute-start
  767.5 277.2 %reduce-scatter.7.cloned.1.call-start = ((), (), s32[]{:S(2)}) async-start(), calls=%async_computation.5 | async-start | bytes 1531904
  781.6 115.9 %collective-permute-start.3 = (f32[3,2816]{1,0:T(4,128)S(1)}, f32[3,2816]{1,0:T(4,128)S(1)}, u32[]{:S(2)}, u32[]{:S(2)}) collective-permute-start(f32[3,2816]{1,0:T(4,128)S(1)} %copy.775), channel_id=1, source_target_pairs={{1,0},{2,1},{3,2},{4,3},{5,4},{6,5},{7,6},{8,7},{9,8},{10,9},{11,1... | collective-permute-start | bytes 101384 | tf_op jit(solution)/shard_map/ppermute | solution.py:13
  (109 other events, 1956.0 us)
Sparse Core Ops, SparseCore 0:
  46.5 93.5 all-gather.3
  143.1 77.5 all-gather.5
  767.7 139.9 reduce-scatter.4
  911.6 133.0 reduce-scatter.6
where the time goes:
time: 1060 us; the launch traced here: 1050 us
  waiting for transfers between devices  335 us (32%)
  blocking collectives  248 us (23%)
  local copies, waits for them, and re-layouts  192 us (18%)
  starting transfers between devices  148 us (14%)
  other arithmetic  104 us (10%)
  between operations  15 us (1%)
    ppermute x32, waiting for transfers between devices, passed_along(): return lax.ppermute(array, axis, pairs)  162 us
    ppermute x32, starting transfers between devices, passed_along(): return lax.ppermute(array, axis, pairs)  148 us
    unnamed x5, waiting for transfers between devices  128 us
    psum x1, blocking collectives, on_device(): lax.psum(jnp.sum(d_log * (-8.0 * recur_gate), axis=0), ('dp', 'ctx'))  115 us
    slice x30, local copies, waits for them, and re-layouts, block_scan(): lax.associative_scan(combine, (summary_coef, summary_value), reverse=reve...  62.1 us
    all_gather x1, blocking collectives, on_device(): lax.all_gather(packed, 'ctx', axis=1, tiled=True)  55.8 us
    all_gather x1, blocking collectives, on_device(): lax.all_gather(weight_x, 'dp', axis=0, tiled=True)  38.7 us
    all_gather x1, blocking collectives, on_device(): lax.all_gather(weight_a, 'dp', axis=0, tiled=True)  38.4 us
  transfers between devices with their start and end apart: 36, of which 33 were waited for; matrix products, arithmetic and copies ran while one was open for 5% of the time, Pallas kernels for 0%

commit v1 on v0

--- a/solution.py
+++ b/solution.py
@@ -172,7 +172,9 @@
     local_wgrad = grad_heads(conv_b, d_recur, head_width)
     row_part = lax.psum_scatter(local_wgrad, "dp", scatter_dimension=0, tiled=True)
     wgrad = lax.psum_scatter(row_part, "ctx", scatter_dimension=1, tiled=True)
-    rgrad = lax.psum(jnp.sum(d_log * (-8.0 * recur_gate), axis=0), ("dp", "ctx"))
+    rgrad = jnp.sum(
+        lax.all_gather(jnp.sum(d_log * (-8.0 * recur_gate), axis=0), ("dp", "ctx")), axis=0
+    )
     return (grad_in.astype(jnp.bfloat16)[None], wgrad, rgrad)
 
 

time: 1060 us -> 2470 us (2.33)
  the two profiles are of different devices: /device:TPU:8 before, /device:TPU:99 now
where the time goes in v1:
time: 2470 us; the launch traced here: 2460 us
  waiting for transfers between devices  1860 us (75%)
  local copies, waits for them, and re-layouts  190 us (8%)
  starting transfers between devices  146 us (6%)
  blocking collectives  124 us (5%)
  other arithmetic  111 us (4%)
    all_gather x1, waiting for transfers between devices, on_device(): lax.all_gather(jnp.sum(d_log * (-8.0 * recur_gate), axis=0), ('dp', 'ctx'))  1410 us
    reduce_scatter x1, waiting for transfers between devices, on_device(): lax.psum_scatter(local_wgrad, 'dp', scatter_dimension=0, tiled=True)  168 us
    ppermute x32, waiting for transfers between devices, passed_along(): return lax.ppermute(array, axis, pairs)  146 us
    ppermute x32, starting transfers between devices, passed_along(): return lax.ppermute(array, axis, pairs)  146 us
    unnamed x6, waiting for transfers between devices  102 us
    slice x30, local copies, waits for them, and re-layouts, block_scan(): lax.associative_scan(combine, (summary_coef, summary_value), reverse=reve...  61.4 us
  transfers between devices with their start and end apart: 37, of which 35 were waited for; matrix products, arithmetic and copies ran while one was open for 2% of the time, Pallas kernels for 0%

profile of v1, /device:TPU:99, one launch (start us, length us, event | category | flops | bytes accessed | tf_op | source)
XLA Modules:
  0.0 2459.6 jit_solution(16614530690555824027)
XLA Ops:
  7.2 34.5 %all_gather.22 = bf16[256,176]{1,0:T(8,128)(2,1)S(1)} all-gather(bf16[8,176]{1,0:T(8,128)(2,1)} %param.15), channel_id=1, replica_groups=mesh['dp'=32,'ctx'=16] {'dp'}, dimensions={0}, use_global_device_ids=true | all-gather | bytes 92928 | tf_op jit(solution)/shard_map/all_gather | solution.py:106
  43.3 8.8 collective-permute-start.2
  52.1 44.5 %all_gather.24 = bf16[256,176]{1,0:T(8,128)(2,1)S(1)} all-gather(bf16[8,176]{1,0:T(8,128)(2,1)} %param.16), channel_id=1, replica_groups=mesh['dp'=32,'ctx'=16] {'dp'}, dimensions={0}, use_global_device_ids=true | all-gather | bytes 92928 | tf_op jit(solution)/shard_map/all_gather | solution.py:107
  100.8 45.1 %all-gather.1 = bf16[16,176,8]{1,2,0:T(8,128)(2,1)S(1)} all-gather(bf16[1,176,8]{1,2,0:T(8,128)(2,1)S(1)} %bitcast.278), channel_id=1, replica_groups=mesh['dp'=32,'ctx'=16] {'ctx'}, dimensions={0}, use_global_device_ids=true | all-gather | bytes 47872 | tf_op jit(solution)/shard_map/all_gather | solution.py:112
  176.0 39.2 %all-gather.9.cloned.1.call-done = bf16[256,2816]{0,1:T(8,128)(2,1)} async-done(((bf16[256,176]{0,1:T(8,128)(2,1)}), bf16[256,2816]{0,1:T(8,128)(2,1)}) %all-gather.9.cloned.1.call-update) | async-done | bytes 1441808 | tf_op jit(solution)/shard_map/all_gather | solution.py:111
  264.3 9.9 slice.532
  274.2 10.0 slice.525
  284.2 10.0 slice.529
  294.1 10.0 slice.527
  385.6 165.9 %while.21 = (s32[]{:T(128)}, f32[2816]{0:T(1024)S(1)}, f32[128,2816]{1,0:T(8,128)}, f32[128,2816]{1,0:T(8,128)}, s32[]{:T(128)}) while((s32[]{:T(128)}, f32[2816]{0:T(1024)S(1)}, f32[128,2816]{1,0:T(8,128)}, f32[128,2816]{1,0:T(8,128)}, s32[]{:T(128)}) %tuple.183), condition=%wide.region_3.0_spmd, body=%wide.region_2.0_spmd.sunk | while | flops 5634 | bytes 135269 | solution.py:144
  588.7 132.1 %while.20 = (s32[]{:T(128)}, f32[2816]{0:T(1024)S(1)}, f32[2816]{0:T(1024)S(1)}, f32[2816]{0:T(1024)S(1)}, s32[]{:T(128)}) while((s32[]{:T(128)}, f32[2816]{0:T(1024)S(1)}, f32[2816]{0:T(1024)S(1)}, f32[2816]{0:T(1024)S(1)}, s32[]{:T(128)}) %tuple.169), condition=%wide.region_1.0_spmd, body=%wide.region_0.0_spmd.sunk | while | flops 5634 | bytes 90213 | solution.py:156
  647.1 8.2 collective-permute-start
  656.1 8.4 collective-permute-start
  665.4 8.4 collective-permute-start
  674.6 8.4 collective-permute-start
  683.9 8.4 collective-permute-start
  693.1 8.4 collective-permute-start
  702.3 8.4 collective-permute-start
  711.6 8.4 collective-permute-start
  720.9 8.9 multiply_reduce_fusion
  734.6 167.7 %reduce-scatter.5.cloned.1.call-done = f32[8,2816]{1,0:T(8,128)} async-done(((f32[256,2816]{1,0:T(8,128)}), f32[8,2816]{1,0:T(8,128)}) %reduce-scatter.5.cloned.1.call-update) | async-done | bytes 90128 | tf_op jit(solution)/shard_map/reduce_scatter | solution.py:173
  918.3 8.2 collective-permute-start.3
  935.2 102.2 %reduce-scatter.7.cloned.1.call-done = f32[176,8]{1,0:T(8,128)} async-done(((f32[2816,8]{1,0:T(8,128)}), f32[176,8]{1,0:T(8,128)}) %reduce-scatter.7.cloned.1.call-update) | async-done | bytes 5648
  1038.9 1407.8 %all-gather.11.cloned.1.call-done = f32[512,1,2816]{2,1,0:T(1,128)} async-done(((f32[1,1,2816]{2,1,0:T(1,128)}), f32[512,1,2816]{2,1,0:T(1,128)}) %all-gather.11.cloned.1.call-update) | async-done | bytes 5767184 | tf_op jit(solution)/shard_map/all_gather | solution.py:176
  (496 shorter events, 470.3 us)
Async XLA Ops:
  7.2 149.8 %all-gather.7.cloned.1.call-start = ((), (), s32[]{:S(2)}) async-start(), calls=%async_computation.2 | async-start | bytes 1531904 | tf_op jit(solution)/shard_map/all_gather | solution.py:110
  42.5 172.8 %all-gather.9.cloned.1.call-start = ((), (), s32[]{:S(2)}) async-start(), calls=%async_computation.3 | async-start | bytes 1531904 | tf_op jit(solution)/shard_map/all_gather | solution.py:111
  43.3 106.1 %collective-permute-start.2 = (bf16[3,2816]{1,0:T(4,128)(2,1)S(1)}, bf16[3,2816]{1,0:T(4,128)(2,1)S(1)}, u32[]{:S(2)}, u32[]{:S(2)}) collective-permute-start(bf16[3,2816]{1,0:T(4,128)(2,1)S(1)} %slice_bitcast_fusion), channel_id=1, source_target_pairs={{0,1},{1,2},{2,3},{3,4},{4,5},{5,6},{6,7},{7,8},{8,9},{9,10},{10,1... | collective-permute-start | bytes 50696 | tf_op jit(solution)/shard_map/ppermute | solution.py:13
  97.4 804.9 %reduce-scatter.5.cloned.1.call-start = ((), (), s32[]{:S(2)}) async-start(), calls=%async_computation.4 | async-start | bytes 2973696 | tf_op jit(solution)/shard_map/reduce_scatter | solution.py:173
  387.2 9.4 collective-permute-start.1
  398.2 9.4 collective-permute-start.1
  409.3 9.4 collective-permute-start.1
  420.3 9.4 collective-permute-start.1
  431.4 9.4 collective-permute-start.1
  442.4 9.4 collective-permute-start.1
  453.5 9.5 collective-permute-start.1
  464.6 9.5 collective-permute-start.1
  475.7 9.4 collective-permute-start.1
  486.7 9.4 collective-permute-start.1
  497.8 9.4 collective-permute-start.1
  508.8 9.4 collective-permute-start.1
  519.9 9.5 collective-permute-start.1
  531.0 9.4 collective-permute-start.1
  542.0 9.4 collective-permute-start.1
  674.6 9.2 collective-permute-start
  683.9 9.2 collective-permute-start
  734.6 302.8 %reduce-scatter.7.cloned.1.call-start = ((), (), s32[]{:S(2)}) async-start(), calls=%async_computation.6 | async-start | bytes 1531904
  904.9 1541.9 %all-gather.11.cloned.1.call-start = ((), (), s32[]{:S(2)}) async-start(), calls=%async_computation.5 | async-start | bytes 5778432 | tf_op jit(solution)/shard_map/all_gather | solution.py:176
  918.3 9.3 collective-permute-start.3
  (110 other events, 2156.2 us)
Sparse Core Ops, SparseCore 0:
  42.6 92.0 all-gather.6
  137.8 77.4 all-gather.8
  734.7 167.6 reduce-scatter.4
  906.3 131.0 reduce-scatter.6
  1040.0 1406.6 all-gather.10
